TPU v7x, 32 devices: a whole 2x2x4 slice. The times are simulated.
32 devices in a mesh: region: 2 (over x), east: 8 (over z, y), north: 2 (over core).
Axes of the slice: x: 2, y: 2, z: 4, core: 2. Of those that a mesh axis runs over, the one named last changes fastest.
Arguments:
- photos: bfloat16 [1024, 4, 16384], P(('region', 'east', 'north')), parts along dimension 0, may hold values from -6 to 6
- footprint: int32 [1024, 1], P(('region', 'east', 'north')), parts along dimension 0, may hold values from 0 to 15; in each aligned block of 32 rows (0 to 31, 32 to 63, ...) at most 2 rows name the same one
- placement: int32 [1024], P(('region', 'east', 'north')), parts along dimension 0, may hold values from 0 to 15
- mask_rows: int32 [1024, 2], P(('region', 'east', 'north')), parts along dimension 0, may hold values from 0 to 128, as said below
- tile_scale: bfloat16 [1024], P(('region', 'east', 'north')), parts along dimension 0, may hold values from 0.5 to 2
Outputs:
- band_zero: bfloat16 [4, 2048, 4096], P(None, ('region', 'north'), 'east'), parts along dimension 1
- band_one: bfloat16 [4, 1024, 2048], P(None, ('region', 'north'), 'east'), parts along dimension 1
- band_two: bfloat16 [4, 512, 1024], P(None, ('region', 'north'), 'east'), parts along dimension 1
- band_three: bfloat16 [4, 256, 512], P(None, 'region'), parts along dimension 1
- apex: bfloat16 [4, 128, 256], P(None, 'region'), parts along dimension 1
There are 2 independent parts, one for each index of `region`. A program takes and returns all parts, laid end to end along the dimension named above; each array names one. Nothing has to cross between parts.
Inputs may be any that keep to these rules, and one draw needn't show every extreme that they name: `footprint`: among the 32 rows of one device no tile is named more than 2 times. `mask_rows`: each row holds a first row below one past the last row.
All inputs are finite; a program needn't handle non-finite values.
Results may differ from a plain program's by a relative error of at most 0.001.
Values may be sent and summed in bfloat16 or wider, within the bound.
No kernel may reach another device: no remote copies, remote signals or barrier semaphores. Data moves between devices by JAX's collectives and lax.ppermute only.
A program may use at most 128 MiB of HBM per device.

v0:
```python
import jax
import jax.numpy as jnp
from jax import lax
from jax.sharding import PartitionSpec as P

BANDS = 4
PATCH = 128
TILE = 512
CAP = 2
BLOCKS = 16
KERNEL = (0.0625, 0.25, 0.375, 0.25, 0.0625)
FLOOR = 0.1
MARGINS = (22, 10, 4, 1)


def padded_2(block, sides, width):
    for axis, dim in sides:
        count = lax.axis_size(axis)
        forward = [(i, i + 1) for i in range(count - 1)]
        backward = [(target, source) for source, target in forward]
        low = lax.ppermute(
            lax.slice_in_dim(block, block.shape[dim] - width, None, axis=dim), axis, forward
        )
        high = lax.ppermute(lax.slice_in_dim(block, 0, width, axis=dim), axis, backward)
        block = jnp.concatenate([low, block, high], axis=dim)
    return block


def tap_table(offset, scale):
    table = jnp.zeros(offset.shape, jnp.float32)
    for tap_index in range(5):
        table = table + jnp.where(offset == tap_index, scale * KERNEL[tap_index], 0.0)
    return table


def reduce_table(size_in):
    size_out = (size_in - 3) // 2
    out_index = jnp.arange(size_out, dtype=jnp.int32)
    in_index = jnp.arange(size_in, dtype=jnp.int32)
    return tap_table(in_index[None, :] - 2 * out_index[:, None], 1.0)


def expand_table(size_in):
    size_out = 2 * (size_in - 2)
    out_index = jnp.arange(size_out, dtype=jnp.int32)
    in_index = jnp.arange(size_in, dtype=jnp.int32)
    return tap_table(2 * in_index[None, :] - out_index[:, None], 2.0)


def apply_tables(padded, row_table, col_table):
    rows_done = jnp.einsum(
        "ih,chw->ciw",
        row_table,
        padded,
        precision=lax.Precision.HIGHEST,
        preferred_element_type=jnp.float32,
    )
    return jnp.einsum(
        "ciw,jw->cij",
        rows_done,
        col_table,
        precision=lax.Precision.HIGHEST,
        preferred_element_type=jnp.float32,
    )


def reduce_padded(padded):
    return apply_tables(padded, reduce_table(padded.shape[1]), reduce_table(padded.shape[2]))


def expand_padded(padded):
    return apply_tables(padded, expand_table(padded.shape[1]), expand_table(padded.shape[2]))


def normalize(grid_field):
    return grid_field[:-1] / jnp.maximum(grid_field[-1:], FLOOR)


def crop_margin(grid_field, margin, keep):
    cut = margin - keep
    return grid_field[:, cut : grid_field.shape[1] - cut, cut : grid_field.shape[2] - cut]


def mask_region(grid_field, margin, tile_side, north_pos, east_pos, north_count, east_count):
    row_global = north_pos * tile_side + jnp.arange(grid_field.shape[1], dtype=jnp.int32) - margin
    col_global = east_pos * tile_side + jnp.arange(grid_field.shape[2], dtype=jnp.int32) - margin
    row_keep = (row_global >= 0) & (row_global < north_count * tile_side)
    col_keep = (col_global >= 0) & (col_global < east_count * tile_side)
    keep_table = (row_keep[:, None] & col_keep[None, :]).astype(jnp.float32)
    return grid_field * keep_table[None, :, :]


def body(photos, footprint, placement, mask_rows, tile_scale):
    east_count = lax.axis_size("east")
    north_count = lax.axis_size("north")
    owners = east_count * north_count
    photo_count = photos.shape[0]
    slot_total = owners * CAP
    target = footprint[:, 0]
    member_table = (target[:, None] == jnp.arange(owners, dtype=jnp.int32)[None, :]).astype(
        jnp.int32
    )
    earlier_count = jnp.cumsum(member_table, axis=0) - member_table
    place_rank = jnp.sum(earlier_count * member_table, axis=1)
    slot_index = target * CAP + place_rank
    slot_match = slot_index[None, :] == jnp.arange(slot_total, dtype=jnp.int32)[:, None]
    filled = jnp.any(slot_match, axis=1)
    source = jnp.sum(
        jnp.where(slot_match, jnp.arange(photo_count, dtype=jnp.int32)[None, :], 0), axis=1
    )
    record = jnp.stack(
        [
            tile_scale.astype(jnp.float32),
            placement.astype(jnp.float32),
            mask_rows[:, 0].astype(jnp.float32),
            mask_rows[:, 1].astype(jnp.float32),
            jnp.ones((photo_count,), jnp.float32),
        ],
        axis=1,
    ).astype(jnp.bfloat16)
    send_photos = jnp.where(filled[:, None, None], photos[source], jnp.zeros((), jnp.bfloat16))
    send_record = jnp.where(filled[:, None], record[source], jnp.zeros((), jnp.bfloat16))
    got_photos, got_record = (
        lax.all_to_all(send_photos, ("east", "north"), split_axis=0, concat_axis=0, tiled=True),
        lax.all_to_all(send_record, ("east", "north"), split_axis=0, concat_axis=0, tiled=True),
    )
    record_value = got_record.astype(jnp.float32)
    gain_scale = record_value[:, 0]
    block_index = record_value[:, 1].astype(jnp.int32)
    lower_row = record_value[:, 2:3]
    upper_row = record_value[:, 3:4]
    live_flag = record_value[:, 4]
    side_index = jnp.arange(PATCH, dtype=jnp.int32)
    edge_weight = (1 + jnp.minimum(side_index, PATCH - 1 - side_index)).astype(jnp.float32)
    feather = edge_weight[:, None] * edge_weight[None, :] / float((PATCH // 2) ** 2)
    side_float = side_index.astype(jnp.float32)
    inside = ((side_float[None, :] >= lower_row) & (side_float[None, :] < upper_row)).astype(
        jnp.float32
    ) * live_flag[:, None]
    weight = inside[:, :, None] * feather[None, :, :]
    gain_value = gain_scale[:, None, None] * weight
    window_photos = got_photos.reshape(slot_total, BANDS, PATCH, PATCH)
    weighted = window_photos.astype(jnp.float32) * gain_value[:, None, :, :]
    block_match = (block_index[None, :] == jnp.arange(BLOCKS, dtype=jnp.int32)[:, None]).astype(
        jnp.float32
    )
    band_sums = jnp.einsum(
        "bk,kcrs->bcrs",
        block_match,
        weighted,
        precision=lax.Precision.HIGHEST,
        preferred_element_type=jnp.float32,
    )
    weight_sums = jnp.einsum(
        "bk,krs->brs",
        block_match,
        weight,
        precision=lax.Precision.HIGHEST,
        preferred_element_type=jnp.float32,
    )
    summed = jnp.concatenate([band_sums, weight_sums[:, None]], axis=1)
    side_blocks = TILE // PATCH
    strips = []
    for block_row in range(side_blocks):
        strips.append(
            jnp.concatenate(
                [summed[block_row * side_blocks + block_col] for block_col in range(side_blocks)],
                axis=2,
            )
        )
    canvas = jnp.concatenate(strips, axis=1)
    results = []
    east_pos = lax.axis_index("east")
    north_pos = lax.axis_index("north")
    grown = padded_2(canvas, (("east", 2), ("north", 1)), MARGINS[0])
    for depth_step in range(3):
        margin_now = MARGINS[depth_step]
        margin_next = MARGINS[depth_step + 1]
        coarse = reduce_padded(grown)
        coarse = mask_region(
            coarse,
            margin_next,
            TILE >> depth_step + 1,
            north_pos,
            east_pos,
            north_count,
            east_count,
        )
        own_field = crop_margin(grown, margin_now, 0)
        coarse_normal = normalize(crop_margin(coarse, margin_next, 1))
        laplace_band = normalize(own_field) - expand_padded(coarse_normal)
        results.append(laplace_band.astype(jnp.bfloat16))
        grown = coarse
    level_field = crop_margin(grown, MARGINS[3], 0)
    stacked = lax.all_gather(level_field[None], ("east", "north"), axis=0, tiled=True)
    chan_count, tall_size, wide_size = level_field.shape
    whole_field = stacked.reshape(east_count, north_count, chan_count, tall_size, wide_size)
    whole_field = whole_field.transpose(2, 1, 3, 0, 4).reshape(
        chan_count, north_count * tall_size, east_count * wide_size
    )
    top_field = reduce_padded(jnp.pad(whole_field, ((0, 0), (2, 2), (2, 2))))
    top_normal = normalize(top_field)
    band_three = (
        normalize(whole_field) - expand_padded(jnp.pad(top_normal, ((0, 0), (1, 1), (1, 1))))
    ).astype(jnp.bfloat16)
    apex = top_normal.astype(jnp.bfloat16)
    return (results[0], results[1], results[2], band_three, apex)


def solution(mesh):
    return jax.shard_map(
        body,
        mesh=mesh,
        in_specs=(
            P(("region", "east", "north"), None, None),
            P(("region", "east", "north"), None),
            P(("region", "east", "north")),
            P(("region", "east", "north"), None),
            P(("region", "east", "north")),
        ),
        out_specs=(
            P(None, ("region", "north"), "east"),
            P(None, ("region", "north"), "east"),
            P(None, ("region", "north"), "east"),
            P(None, "region", None),
            P(None, "region", None),
        ),
        check_vma=False,
    )
```

profile of v0, /device:TPU:0, one launch (start us, length us, event | category | flops | bytes accessed | tf_op | source)
XLA Modules:
  0.0 301.0 jit_solution(17203847547347885743)
XLA Ops:
  13.3 7.4 %all-to-all-start = ((bf16[16,2,5]{2,1,0:T(2,128)(2,1)}), bf16[16,2,5]{2,1,0:T(2,128)(2,1)S(1)}, u32[]{:S(2)}, u32[]{:S(2)}) async-start(bf16[16,2,5]{2,1,0:T(2,128)(2,1)} %broadcast_select_fusion.1), calls=%async_computation | async-start | bytes 16384 | tf_op jit(solution)/shard_map/all_to_all | solution.py:125
  20.7 8.0 %gather_fusion.1 = bf16[32,4,16384]{2,1,0:T(4,128)(2,1)} fusion(bf16[32,4,16384]{2,1,0:T(4,128)(2,1)} %param.5, s32[1024]{0:T(1024)S(1)} %pad_clamp_fusion), kind=kCustom, calls=%fused_computation.1 | custom fusion | bytes 8388736 | tf_op jit(solution)/shard_map/gather | solution.py:121
  28.7 5.9 %broadcast_select_fusion = bf16[32,4,16384]{2,1,0:T(4,128)(2,1)} fusion(bf16[32,4,16384]{2,1,0:T(4,128)(2,1)} %gather_fusion.1, pred[32]{0:T(512)(128)(4,1)S(1)} %fusion.201), kind=kLoop, calls=%fused_computation.80 | loop fusion | flops 2097152 | bytes 8388640 | tf_op jit(solution)/shard_map/jit(_where)/select_n | solution.py:121
  34.6 6.1 %all-to-all-start.1 = ((bf16[32,4,16384]{2,1,0:T(4,128)(2,1)}), bf16[32,4,16384]{2,1,0:T(4,128)(2,1)}, u32[]{:S(2)}, u32[]{:S(2)}) async-start(bf16[32,4,16384]{2,1,0:T(4,128)(2,1)} %broadcast_select_fusion), calls=%async_computation.1 | async-start | bytes 8388608 | tf_op jit(solution)/shard_map/all_to_all | solution.py:124
  42.6 2.1 fusion.58
  45.3 73.0 %all-to-all-done.1 = bf16[32,4,16384]{2,1,0:T(4,128)(2,1)} async-done(((bf16[32,4,16384]{2,1,0:T(4,128)(2,1)}), bf16[32,4,16384]{2,1,0:T(4,128)(2,1)}, u32[]{:S(2)}, u32[]{:S(2)}) %all-to-all-start.1) | async-done | bytes 4194336 | tf_op jit(solution)/shard_map/all_to_all | solution.py:124
  118.3 8.9 %reshape.371 = f32[32,4,128,128]{3,2,1,0:T(8,128)} reshape(bf16[32,4,16384]{2,1,0:T(4,128)(2,1)} %all-to-all-done.1) | data formatting | bytes 12582912 | tf_op jit(solution)/shard_map/convert_element_type | solution.py:143
  127.3 10.9 %fusion = f32[16,4,128,128]{3,0,2,1:T(8,128)S(1)} fusion(f32[32,4,128,128]{3,2,1,0:T(8,128)} %reshape.371, f32[32,128,128]{2,0,1:T(8,128)S(1)} %multiply_multiply_fusion, s32[32]{0:T(128)S(1)} %fusion.200), kind=kOutput, calls=%fused_computation.18 | convolution fusion | flops 404750848 | bytes 14680192 | tf_op jit(solution)/shard_map/bk,kcrs->bcrs/dot_general | solution.py:147
  138.2 2.8 fusion.110
  140.9 2.7 fusion.119
  143.8 1.7 maximum_maximum_fusion.2
  146.6 2.4 copy.121
  149.0 8.8 %collective-permute-start = (f32[5,512,22]{1,2,0:T(8,128)}, f32[5,512,22]{1,2,0:T(8,128)}, u32[]{:S(2)}, u32[]{:S(2)}) collective-permute-start(f32[5,512,22]{1,2,0:T(8,128)} %copy.121), channel_id=1, source_target_pairs={{0,2},{2,4},{4,6},{6,8},{8,10},{10,12},{12,14},{1,3},{3,5},{5,7},{... | collective-permute-start | bytes 675848 | tf_op jit(solution)/shard_map/ppermute | solution.py:21
  157.8 2.4 copy.122
  161.6 2.0 collective-permute-done
  163.5 2.5 copy.123
  166.0 11.5 %collective-permute-done.1 = f32[5,512,22]{1,2,0:T(8,128)} collective-permute-done((f32[5,512,22]{1,2,0:T(8,128)}, f32[5,512,22]{1,2,0:T(8,128)}, u32[]{:S(2)}, u32[]{:S(2)}) %collective-permute-start.1) | collective-permute-done | bytes 225312 | tf_op jit(solution)/shard_map/ppermute | solution.py:24
  177.5 2.4 copy.124
  179.9 12.6 %pad_maximum_fusion = f32[5,512,556]{2,1,0:T(8,128)S(1)} fusion(f32[5,512,22]{2,1,0:T(8,128)} %copy.124, f32[5,128,128]{2,1,0:T(8,128)} %bitcast.251, f32[5,128,128]{2,1,0:T(8,128)} %bitcast.257, f32[5,128,128]{2,1,0:T(8,128)} %bitcast.245, f32[5,128,128]{2,1,0:T(8,128)} %bitcast.239, f32[5,128,128]{2,1,0:T(8,128)} %bitcast.233, ...), kind=kLoop, calls=%fused_computation.74 | loop fusion | flops 24197120 | bytes 11386880 | tf_op jit(solution)/shard_map/concatenate | solution.py:25
  195.3 3.5 %maximum_maximum_fusion = f32[5,512,512]{2,1,0:T(8,128)} fusion(f32[5,128,128]{2,1,0:T(8,128)S(1)} %bitcast.252, f32[5,128,128]{2,1,0:T(8,128)S(1)} %bitcast.258, f32[5,128,128]{2,1,0:T(8,128)S(1)} %bitcast.246, f32[5,128,128]{2,1,0:T(8,128)S(1)} %bitcast.240, f32[5,128,128]{2,1,0:T(8,128)S(1)} %bitcast.234, f32[5,128,128]{2,1,0:T(8,128)S(1)} %bitcast.228, ...), kind=kLoop, calls=%fused_computation.75 | loop fusion | flops 19660800 | bytes 10485760 | tf_op jit(solution)/shard_map/concatenate | solution.py:171
  201.0 12.4 %fusion.1 = f32[5,556,276]{1,2,0:T(8,128)S(1)} fusion(f32[5,22,556]{2,1,0:T(8,128)S(1)} %collective-permute-done.3, f32[5,512,22]{2,1,0:T(8,128)S(1)} %copy-done.15, f32[5,128,128]{2,1,0:T(8,128)S(1)} %bitcast.254, f32[5,128,128]{2,1,0:T(8,128)S(1)} %bitcast.260, f32[5,128,128]{2,1,0:T(8,128)S(1)} %bitcast.248, f32[5,128,128]{2,1,0:T(8,128)S(1)} %bitcast.242, ...), kind=kOutput, calls=%fused_computation.34 | convolution fusion | flops 5150962176 | bytes 9252944 | tf_op jit(solution)/shard_map/ih,chw->ciw/dot_general | solution.py:51
  213.4 7.4 %fusion.54 = f32[5,276,276]{2,1,0:T(8,128)S(1)} fusion(f32[5,556,276]{1,2,0:T(8,128)S(1)} %fusion.1, f32[276,276]{1,0:T(8,128)S(1)} %copy-done.17, s32[276]{0:T(512)S(1)} %iota_multiply_fusion.1), kind=kOutput, calls=%fused_computation.91 | convolution fusion | flops 2543913984 | bytes 4898448 | tf_op jit(solution)/shard_map/ciw,jw->cij/dot_general | solution.py:58
  220.8 2.3 convolution_bitcast_fusion
  224.4 1.7 convolution_bitcast_fusion.3
  232.1 2.9 fusion.64
  235.0 4.5 %fusion.57 = f32[4,258,512]{2,1,0:T(8,128)S(1)} fusion(f32[5,276,276]{2,1,0:T(8,128)S(1)} %fusion.54, f32[258,258]{1,0:T(8,128)S(1)} %fusion.108, s32[258]{0:T(512)S(1)} %iota_multiply_fusion), kind=kOutput, calls=%fused_computation.93 | convolution fusion | flops 1638124544 | bytes 4143104 | tf_op jit(solution)/shard_map/ih,chw->ciw/dot_general | solution.py:51
  239.6 9.1 %fusion.42 = bf16[4,512,512]{2,1,0:T(8,128)(2,1)} fusion(f32[5,512,512]{2,1,0:T(8,128)S(1)} %bitcast.262, f32[512,512]{1,0:T(8,128)S(1)} %copy-done.18, f32[4,258,512]{2,1,0:T(8,128)S(1)} %fusion.57, s32[258]{0:T(512)S(1)} %iota_multiply_fusion), kind=kOutput, calls=%fused_computation.78 | convolution fusion | flops 3251518464 | bytes 9454600 | tf_op jit(solution)/shard_map/ciw,jw->cij/dot_general | solution.py:58
  248.7 26.4 %all-gather.3.cloned.1.call-done = f32[80,64,64]{2,1,0:T(8,128)} async-done(((f32[5,64,64]{2,1,0:T(8,128)}), f32[80,64,64]{2,1,0:T(8,128)}) %all-gather.3.cloned.1.call-update) | async-done | bytes 1310736 | tf_op jit(solution)/shard_map/all_gather | solution.py:195
  275.1 3.4 %copy.153 = f32[8,2,5,64,64]{4,0,3,1,2:T(8,128)S(1)} copy(f32[8,2,5,64,64]{4,3,2,1,0:T(8,128)} %bitcast.263) | data formatting | bytes 2621440 | tf_op jit(solution)/shard_map/reshape | solution.py:197
  278.5 1.7 reshape.369
  285.5 2.2 convolution_bitcast_fusion.2
  289.3 4.4 %fusion.65 = bf16[4,128,512]{2,1,0:T(8,128)(2,1)} fusion(f32[4,128,258]{1,2,0:T(8,128)} %convolution_bitcast_fusion.2, f32[4,128,512]{2,1,0:T(8,128)} %slice.198, f32[128,512]{1,0:T(8,128)S(1)} %max.70, s32[258]{0:T(512)S(1)} %iota_multiply_fusion), kind=kOutput, calls=%fused_computation.102 | convolution fusion | flops 814365696 | bytes 2364424 | tf_op jit(solution)/shard_map/ciw,jw->cij/dot_general | solution.py:58
  (110 shorter events, 30.0 us)
Async XLA Ops:
  13.3 21.3 %all-to-all-start = ((bf16[16,2,5]{2,1,0:T(2,128)(2,1)}), bf16[16,2,5]{2,1,0:T(2,128)(2,1)S(1)}, u32[]{:S(2)}, u32[]{:S(2)}) async-start(bf16[16,2,5]{2,1,0:T(2,128)(2,1)} %broadcast_select_fusion.1), calls=%async_computation | async-start | bytes 16384 | tf_op jit(solution)/shard_map/all_to_all | solution.py:125
  34.6 83.7 %all-to-all-start.1 = ((bf16[32,4,16384]{2,1,0:T(4,128)(2,1)}), bf16[32,4,16384]{2,1,0:T(4,128)(2,1)}, u32[]{:S(2)}, u32[]{:S(2)}) async-start(bf16[32,4,16384]{2,1,0:T(4,128)(2,1)} %broadcast_select_fusion), calls=%async_computation.1 | async-start | bytes 8388608 | tf_op jit(solution)/shard_map/all_to_all | solution.py:124
  40.7 234.4 %all-gather.3.cloned.1.call-start = ((), (), s32[]{:S(2)}) async-start(), calls=%async_computation.2 | async-start | bytes 2785280 | tf_op jit(solution)/shard_map/all_gather | solution.py:195
  127.3 10.9 %copy-start.12 = (f32[16,1,128,128]{3,0,2,1:T(8,128)S(1)}, f32[16,1,128,128]{3,0,2,1:T(8,128)}, u32[]{:S(2)}) copy-start(f32[16,1,128,128]{3,0,2,1:T(8,128)} %fusion.58) | copy-start | bytes 3145732
  143.7 1.7 copy-start
  143.7 1.7 copy-start.2
  143.7 1.7 copy-start.4
  143.7 1.7 copy-start.6
  143.7 1.7 copy-start.8
  143.7 1.7 copy-start.10
  149.0 14.5 %collective-permute-start = (f32[5,512,22]{1,2,0:T(8,128)}, f32[5,512,22]{1,2,0:T(8,128)}, u32[]{:S(2)}, u32[]{:S(2)}) collective-permute-start(f32[5,512,22]{1,2,0:T(8,128)} %copy.121), channel_id=1, source_target_pairs={{0,2},{2,4},{4,6},{6,8},{8,10},{10,12},{12,14},{1,3},{3,5},{5,7},{... | collective-permute-start | bytes 675848 | tf_op jit(solution)/shard_map/ppermute | solution.py:21
  160.2 17.3 %collective-permute-start.1 = (f32[5,512,22]{1,2,0:T(8,128)}, f32[5,512,22]{1,2,0:T(8,128)}, u32[]{:S(2)}, u32[]{:S(2)}) collective-permute-start(f32[5,512,22]{1,2,0:T(8,128)} %copy.122), channel_id=1, source_target_pairs={{2,0},{4,2},{6,4},{8,6},{10,8},{12,10},{14,12},{3,1},{5,3},{7,5},{... | collective-permute-start | bytes 675848 | tf_op jit(solution)/shard_map/ppermute | solution.py:24
  179.9 15.4 %copy-start.1 = (f32[1,5,128,128]{3,0,2,1:T(1,128)S(1)}, f32[1,5,128,128]{3,0,2,1:T(1,128)}, u32[]{:S(2)}) copy-start(f32[1,5,128,128]{3,0,2,1:T(1,128)} %copy-done) | copy-start | bytes 983044
  179.9 15.4 %copy-start.3 = (f32[1,5,128,128]{3,0,2,1:T(1,128)S(1)}, f32[1,5,128,128]{3,0,2,1:T(1,128)}, u32[]{:S(2)}) copy-start(f32[1,5,128,128]{3,0,2,1:T(1,128)} %copy-done.2) | copy-start | bytes 983044
  179.9 15.4 %copy-start.5 = (f32[1,5,128,128]{3,0,2,1:T(1,128)S(1)}, f32[1,5,128,128]{3,0,2,1:T(1,128)}, u32[]{:S(2)}) copy-start(f32[1,5,128,128]{3,0,2,1:T(1,128)} %copy-done.4) | copy-start | bytes 983044
  179.9 15.4 %copy-start.7 = (f32[1,5,128,128]{3,0,2,1:T(1,128)S(1)}, f32[1,5,128,128]{3,0,2,1:T(1,128)}, u32[]{:S(2)}) copy-start(f32[1,5,128,128]{3,0,2,1:T(1,128)} %copy-done.6) | copy-start | bytes 983044
  179.9 15.4 %copy-start.9 = (f32[1,5,128,128]{3,0,2,1:T(1,128)S(1)}, f32[1,5,128,128]{3,0,2,1:T(1,128)}, u32[]{:S(2)}) copy-start(f32[1,5,128,128]{3,0,2,1:T(1,128)} %copy-done.8) | copy-start | bytes 983044
  179.9 15.4 %copy-start.11 = (f32[1,5,128,128]{3,0,2,1:T(1,128)S(1)}, f32[1,5,128,128]{3,0,2,1:T(1,128)}, u32[]{:S(2)}) copy-start(f32[1,5,128,128]{3,0,2,1:T(1,128)} %copy-done.10) | copy-start | bytes 983044
  192.7 7.5 %collective-permute-start.2 = (f32[5,22,556]{2,1,0:T(8,128)S(1)}, f32[5,22,556]{2,1,0:T(8,128)S(1)}, u32[]{:S(2)}, u32[]{:S(2)}) collective-permute-start(f32[5,22,556]{2,1,0:T(8,128)S(1)} %get-tuple-element.11), channel_id=1, source_target_pairs={{0,1},{2,3},{4,5},{6,7},{8,9},{10,11},{12,13},{14,15},{16,17},{18,... | collective-permute-start | bytes 733928 | tf_op jit(solution)/shard_map/ppermute | solution.py:21
  194.0 6.1 %collective-permute-start.3 = (f32[5,22,556]{2,1,0:T(8,128)S(1)}, f32[5,22,556]{2,1,0:T(8,128)S(1)}, u32[]{:S(2)}, u32[]{:S(2)}) collective-permute-start(f32[5,22,556]{2,1,0:T(8,128)S(1)} %get-tuple-element.12), channel_id=1, source_target_pairs={{1,0},{3,2},{5,4},{7,6},{9,8},{11,10},{13,12},{15,14},{17,16},{19,... | collective-permute-start | bytes 733928 | tf_op jit(solution)/shard_map/ppermute | solution.py:24
  198.9 1.7 copy-start.14
  198.9 2.1 copy-start.15
  200.1 13.2 %copy-start.17 = (f32[276,276]{1,0:T(8,128)S(1)}, f32[276,276]{1,0:T(8,128)}, u32[]{:S(2)}) copy-start(f32[276,276]{1,0:T(8,128)} %and_convert_fusion) | copy-start | bytes 914116
  232.1 7.4 %slice-start = ((s8[5242880]{0:T(1024)(128)(4,1)}), s8[4194304]{0:T(1024)(128)(4,1)S(1)}, s32[]{:S(2)}) async-start(s8[5242880]{0:T(1024)(128)(4,1)} %bitcast.261), calls=%async_computation.3 | async-start | bytes 8388608
  235.0 4.6 %slice-start.1 = ((s8[5242880]{0:T(1024)(128)(4,1)}), s8[1048576]{0:T(1024)(128)(4,1)S(1)}, s32[]{:S(2)}) async-start(s8[5242880]{0:T(1024)(128)(4,1)} %bitcast.261), calls=%async_computation.4 | async-start | bytes 2097152
  235.0 4.6 %copy-start.18 = (f32[512,512]{1,0:T(8,128)S(1)}, f32[512,512]{1,0:T(8,128)}, u32[]{:S(2)}) copy-start(f32[512,512]{1,0:T(8,128)} %fusion.67) | copy-start | bytes 3145732
  280.1 1.9 copy-start.16
  282.0 5.7 %copy-start.13 = (f32[4,2,64,8,64]{4,3,2,1,0:T(8,128)S(1)}, f32[4,2,64,8,64]{4,3,2,1,0:T(8,128)}, u32[]{:S(2)}) copy-start(f32[4,2,64,8,64]{4,3,2,1,0:T(8,128)} %slice.255) | copy-start | bytes 3145732
Sparse Core Ops, SparseCore 0:
  228.6 46.4 all-gather.2
where the time goes:
time: 306 us; the launch traced here: 301 us
  waiting for transfers between devices  113 us (37%)
  matrix products  68.6 us (22%)
  other arithmetic  39.6 us (13%)
  local copies, waits for them, and re-layouts  38.5 us (13%)
  starting transfers between devices  26.4 us (9%)
  between operations  15 us (5%)
    all_to_all x1, waiting for transfers between devices, body(): lax.all_to_all(send_photos, ('east', 'north'), split_axis=0, concat_axis=...  73 us
    dot_general x8, matrix products, apply_tables(): jnp.einsum('ciw,jw->cij', rows_done, col_table, precision=lax.Precision.H...  28.9 us
    dot_general x8, matrix products, apply_tables(): jnp.einsum('ih,chw->ciw', row_table, padded, precision=lax.Precision.HIGH...  26.7 us
    all_gather x1, waiting for transfers between devices, body(): lax.all_gather(level_field[None], ('east', 'north'), axis=0, tiled=True)  26.4 us
    concatenate x1, other arithmetic, padded_2(): block = jnp.concatenate([low, block, high], axis=dim)  12.6 us
    ppermute x2, waiting for transfers between devices, padded_2(): lax.ppermute(lax.slice_in_dim(block, 0, width, axis=dim), axis, backward)  11.5 us
    dot_general x1, matrix products, body(): jnp.einsum('bk,kcrs->bcrs', block_match, weighted, precision=lax.Precisio...  10.9 us
    ppermute x2, starting transfers between devices, padded_2(): lax.ppermute(lax.slice_in_dim(block, block.shape[dim] - width, None, axis...  10.1 us
  transfers between devices with their start and end apart: 7, of which 4 were waited for; matrix products, arithmetic and copies ran while one was open for 16% of the time, Pallas kernels for 0%

commit v1 on v0

--- a/solution.py
+++ b/solution.py
@@ -11,6 +11,22 @@
 KERNEL = (0.0625, 0.25, 0.375, 0.25, 0.0625)
 FLOOR = 0.1
 MARGINS = (22, 10, 4, 1)
+
+
+def collect(x, axis, dim):
+    ways, here, turn = (lax.axis_size(axis), lax.axis_index(axis), x.shape[dim])
+    shape = [n * ways if d == dim else n for d, n in enumerate(x.shape)]
+    full = lax.dynamic_update_slice_in_dim(jnp.zeros(shape, x.dtype), x, here * turn, axis=dim)
+    going_up = going_down = x
+    for far in range(1, ways // 2 + 1):
+        going_up = lax.ppermute(going_up, axis, [(d, (d + 1) % ways) for d in range(ways)])
+        full = lax.dynamic_update_slice_in_dim(full, going_up, (here - far) % ways * turn, axis=dim)
+        if 2 * far < ways:
+            going_down = lax.ppermute(going_down, axis, [(d, (d - 1) % ways) for d in range(ways)])
+            full = lax.dynamic_update_slice_in_dim(
+                full, going_down, (here + far) % ways * turn, axis=dim
+            )
+    return full
 
 
 def padded_2(block, sides, width):
@@ -192,7 +208,7 @@
         results.append(laplace_band.astype(jnp.bfloat16))
         grown = coarse
     level_field = crop_margin(grown, MARGINS[3], 0)
-    stacked = lax.all_gather(level_field[None], ("east", "north"), axis=0, tiled=True)
+    stacked = collect(level_field[None], ("east", "north"), 0)
     chan_count, tall_size, wide_size = level_field.shape
     whole_field = stacked.reshape(east_count, north_count, chan_count, tall_size, wide_size)
     whole_field = whole_field.transpose(2, 1, 3, 0, 4).reshape(

time: 306 us -> 321 us (1.049)
  starting transfers between devices: 26.4 us -> 58.2 us
  between operations: 15 us -> 1.84 us
  other arithmetic: 39.6 us -> 35.6 us
    ppermute x0 -> x15, starting transfers between devices: none -> 31.6 us  [the longest x7 30.1 us: collect(): lax.ppermute(going_down, axis, [(d, (d - 1) % ways) for d in range(ways)])]
    all_gather x1 -> x0, waiting for transfers between devices: 26.4 us -> none  [body(): lax.all_gather(level_field[None], ('east', 'north'), axis=0, tiled=True)]
    ppermute x0 -> x15, waiting for transfers between devices: none -> 25.4 us  [the longest x8 25.4 us: collect(): lax.ppermute(going_up, axis, [(d, (d + 1) % ways) for d in range(ways)])]
    reshape x1 -> x0, local copies, waits for them, and re-layouts: 3.38 us -> none  [body(): stacked.reshape(east_count, north_count, chan_count, tall_size, wide_size)]
  transfers between devices with their start and end apart: 7 -> 21, of which waited for: 4 -> 11; matrix products, arithmetic and copies ran while one was open for 16% -> 14% of each run, Pallas kernels for 0% -> 0%
where the time goes in v1:
time: 321 us; the launch traced here: 316 us
  waiting for transfers between devices  113 us (35%)
  matrix products  70.2 us (22%)
  starting transfers between devices  58.2 us (18%)
  local copies, waits for them, and re-layouts  37.3 us (12%)
  other arithmetic  35.6 us (11%)
    all_to_all x1, waiting for transfers between devices, body(): lax.all_to_all(send_photos, ('east', 'north'), split_axis=0, concat_axis=...  73 us
    ppermute x7, starting transfers between devices, collect(): lax.ppermute(going_down, axis, [(d, (d - 1) % ways) for d in range(ways)])  30.1 us
    dot_general x8, matrix products, apply_tables(): jnp.einsum('ciw,jw->cij', rows_done, col_table, precision=lax.Precision.H...  29.1 us
    dot_general x8, matrix products, apply_tables(): jnp.einsum('ih,chw->ciw', row_table, padded, precision=lax.Precision.HIGH...  28.1 us
    ppermute x8, waiting for transfers between devices, collect(): lax.ppermute(going_up, axis, [(d, (d + 1) % ways) for d in range(ways)])  25.4 us
    ppermute x2, waiting for transfers between devices, padded_2(): lax.ppermute(lax.slice_in_dim(block, 0, width, axis=dim), axis, backward)  12.8 us
    concatenate x1, other arithmetic, padded_2(): block = jnp.concatenate([low, block, high], axis=dim)  12.6 us
    dot_general x1, matrix products, body(): jnp.einsum('bk,kcrs->bcrs', block_match, weighted, precision=lax.Precisio...  10.9 us
  transfers between devices with their start and end apart: 21, of which 11 were waited for; matrix products, arithmetic and copies ran while one was open for 14% of the time, Pallas kernels for 0%

profile of v1, /device:TPU:0, one launch (start us, length us, event | category | flops | bytes accessed | tf_op | source)
XLA Modules:
  0.0 316.2 jit_solution(17073846073351647327)
XLA Ops:
  6.8 7.4 %all-to-all-start = ((bf16[16,2,5]{2,1,0:T(2,128)(2,1)}), bf16[16,2,5]{2,1,0:T(2,128)(2,1)S(1)}, u32[]{:S(2)}, u32[]{:S(2)}) async-start(bf16[16,2,5]{2,1,0:T(2,128)(2,1)} %broadcast_select_fusion.1), calls=%async_computation | async-start | bytes 16384 | tf_op jit(solution)/shard_map/all_to_all | solution.py:141
  14.2 7.9 %gather_fusion.1 = bf16[32,4,16384]{2,1,0:T(4,128)(2,1)} fusion(bf16[32,4,16384]{2,1,0:T(4,128)(2,1)} %param.5, s32[1024]{0:T(1024)S(1)} %pad_clamp_fusion), kind=kCustom, calls=%fused_computation.1 | custom fusion | bytes 8388736 | tf_op jit(solution)/shard_map/gather | solution.py:137
  22.1 5.9 %broadcast_select_fusion = bf16[32,4,16384]{2,1,0:T(4,128)(2,1)} fusion(bf16[32,4,16384]{2,1,0:T(4,128)(2,1)} %gather_fusion.1, pred[32]{0:T(512)(128)(4,1)S(1)} %fusion.201), kind=kLoop, calls=%fused_computation.80 | loop fusion | flops 2097152 | bytes 8388640 | tf_op jit(solution)/shard_map/jit(_where)/select_n | solution.py:137
  28.0 6.5 %all-to-all-start.1 = ((bf16[32,4,16384]{2,1,0:T(4,128)(2,1)}), bf16[32,4,16384]{2,1,0:T(4,128)(2,1)}, u32[]{:S(2)}, u32[]{:S(2)}) async-start(bf16[32,4,16384]{2,1,0:T(4,128)(2,1)} %broadcast_select_fusion), calls=%async_computation.1 | async-start | bytes 8388608 | tf_op jit(solution)/shard_map/all_to_all | solution.py:140
  39.2 73.0 %all-to-all-done.1 = bf16[32,4,16384]{2,1,0:T(4,128)(2,1)} async-done(((bf16[32,4,16384]{2,1,0:T(4,128)(2,1)}), bf16[32,4,16384]{2,1,0:T(4,128)(2,1)}, u32[]{:S(2)}, u32[]{:S(2)}) %all-to-all-start.1) | async-done | bytes 4194336 | tf_op jit(solution)/shard_map/all_to_all | solution.py:140
  112.2 9.0 %reshape.371 = f32[32,4,128,128]{3,2,1,0:T(8,128)} reshape(bf16[32,4,16384]{2,1,0:T(4,128)(2,1)} %all-to-all-done.1) | data formatting | bytes 12582912 | tf_op jit(solution)/shard_map/convert_element_type | solution.py:159
  121.2 10.9 %fusion = f32[16,4,128,128]{3,0,2,1:T(8,128)S(1)} fusion(f32[32,4,128,128]{3,2,1,0:T(8,128)} %reshape.371, f32[32,128,128]{2,0,1:T(8,128)S(1)} %multiply_multiply_fusion, s32[32]{0:T(128)S(1)} %fusion.200), kind=kOutput, calls=%fused_computation.18 | convolution fusion | flops 404750848 | bytes 14680192 | tf_op jit(solution)/shard_map/bk,kcrs->bcrs/dot_general | solution.py:163
  132.1 2.8 fusion.110
  142.9 8.8 %collective-permute-start = (f32[5,512,22]{1,2,0:T(8,128)}, f32[5,512,22]{1,2,0:T(8,128)}, u32[]{:S(2)}, u32[]{:S(2)}) collective-permute-start(f32[5,512,22]{1,2,0:T(8,128)} %copy.124), channel_id=1, source_target_pairs={{0,2},{2,4},{4,6},{6,8},{8,10},{10,12},{12,14},{1,3},{3,5},{5,7},{... | collective-permute-start | bytes 675848 | tf_op jit(solution)/shard_map/ppermute | solution.py:37
  159.9 11.5 %collective-permute-done.1 = f32[5,512,22]{1,2,0:T(8,128)} collective-permute-done((f32[5,512,22]{1,2,0:T(8,128)}, f32[5,512,22]{1,2,0:T(8,128)}, u32[]{:S(2)}, u32[]{:S(2)}) %collective-permute-start.1) | collective-permute-done | bytes 225312 | tf_op jit(solution)/shard_map/ppermute | solution.py:40
  173.8 12.6 %pad_maximum_fusion = f32[5,512,556]{2,1,0:T(8,128)S(1)} fusion(f32[5,512,22]{2,1,0:T(8,128)} %copy.127, f32[5,128,128]{2,1,0:T(8,128)} %bitcast.254, f32[5,128,128]{2,1,0:T(8,128)} %bitcast.260, f32[5,128,128]{2,1,0:T(8,128)} %bitcast.248, f32[5,128,128]{2,1,0:T(8,128)} %bitcast.242, f32[5,128,128]{2,1,0:T(8,128)} %bitcast.236, ...), kind=kLoop, calls=%fused_computation.74 | loop fusion | flops 24197120 | bytes 11386880 | tf_op jit(solution)/shard_map/concatenate | solution.py:41
  191.6 12.3 %fusion.1 = f32[5,556,276]{1,2,0:T(8,128)S(1)} fusion(f32[5,22,556]{2,1,0:T(8,128)S(1)} %collective-permute-done.3, f32[5,512,22]{2,1,0:T(8,128)S(1)} %copy-done.15, f32[5,128,128]{2,1,0:T(8,128)S(1)} %bitcast.257, f32[5,128,128]{2,1,0:T(8,128)S(1)} %bitcast.263, f32[5,128,128]{2,1,0:T(8,128)S(1)} %bitcast.251, f32[5,128,128]{2,1,0:T(8,128)S(1)} %bitcast.245, ...), kind=kOutput, calls=%fused_computation.34 | convolution fusion | flops 5150962176 | bytes 9252944 | tf_op jit(solution)/shard_map/ih,chw->ciw/dot_general | solution.py:67
  204.0 7.8 %fusion.54 = f32[5,276,276]{2,1,0:T(8,128)S(1)} fusion(f32[5,556,276]{1,2,0:T(8,128)S(1)} %fusion.1, f32[276,276]{1,0:T(8,128)S(1)} %copy-done.16, s32[276]{0:T(512)S(1)} %iota_multiply_fusion.1), kind=kOutput, calls=%fused_computation.90 | convolution fusion | flops 2543913984 | bytes 4898448 | tf_op jit(solution)/shard_map/ciw,jw->cij/dot_general | solution.py:74
  219.7 3.4 %collective-permute-start.5 = (f32[1,5,64,64]{3,2,1,0:T(8,128)S(1)}, f32[1,5,64,64]{3,2,1,0:T(8,128)S(1)}, u32[]{:S(2)}, u32[]{:S(2)}) collective-permute-start(f32[1,5,64,64]{3,2,1,0:T(8,128)S(1)} %slice_bitcast_fusion), channel_id=1, source_target_pairs={{0,15},{1,0},{2,1},{3,2},{4,3},{5,4},{6,5},{7,6},{8,7},{9,8},{10,9... | collective-permute-start | bytes 245768 | tf_op jit(solution)/shard_map/ppermute | solution.py:25
  227.0 3.0 fusion.64
  229.9 4.5 %fusion.57 = f32[4,258,512]{2,1,0:T(8,128)S(1)} fusion(f32[5,276,276]{2,1,0:T(8,128)S(1)} %fusion.54, f32[258,258]{1,0:T(8,128)S(1)} %fusion.108, s32[258]{0:T(512)S(1)} %iota_multiply_fusion), kind=kOutput, calls=%fused_computation.92 | convolution fusion | flops 1638124544 | bytes 4143104 | tf_op jit(solution)/shard_map/ih,chw->ciw/dot_general | solution.py:67
  234.5 8.8 %fusion.42 = bf16[4,512,512]{2,1,0:T(8,128)(2,1)} fusion(f32[5,512,512]{2,1,0:T(8,128)S(1)} %maximum_maximum_fusion, f32[512,512]{1,0:T(8,128)S(1)} %fusion.67, f32[4,258,512]{2,1,0:T(8,128)S(1)} %fusion.57, s32[258]{0:T(512)S(1)} %iota_multiply_fusion), kind=kOutput, calls=%fused_computation.78 | convolution fusion | flops 3251518464 | bytes 9454600 | tf_op jit(solution)/shard_map/ciw,jw->cij/dot_general | solution.py:74
  243.8 4.4 %collective-permute-start.7 = (f32[1,5,64,64]{3,2,1,0:T(8,128)S(1)}, f32[1,5,64,64]{3,2,1,0:T(8,128)S(1)}, u32[]{:S(2)}, u32[]{:S(2)}) collective-permute-start(f32[1,5,64,64]{3,2,1,0:T(8,128)S(1)} %collective-permute-done.5), channel_id=1, source_target_pairs={{0,15},{1,0},{2,1},{3,2},{4,3},{5,4},{6,5},{7,6},{8,7},{9,8},{10,9... | collective-permute-start | bytes 245768 | tf_op jit(solution)/shard_map/ppermute | solution.py:25
  248.3 3.1 collective-permute-done.6
  251.4 4.4 %collective-permute-start.9 = (f32[1,5,64,64]{3,2,1,0:T(8,128)S(1)}, f32[1,5,64,64]{3,2,1,0:T(8,128)S(1)}, u32[]{:S(2)}, u32[]{:S(2)}) collective-permute-start(f32[1,5,64,64]{3,2,1,0:T(8,128)S(1)} %collective-permute-done.7), channel_id=1, source_target_pairs={{0,15},{1,0},{2,1},{3,2},{4,3},{5,4},{6,5},{7,6},{8,7},{9,8},{10,9... | collective-permute-start | bytes 245768 | tf_op jit(solution)/shard_map/ppermute | solution.py:25
  255.9 2.9 collective-permute-done.8
  258.8 4.5 %collective-permute-start.11 = (f32[1,5,64,64]{3,2,1,0:T(8,128)S(1)}, f32[1,5,64,64]{3,2,1,0:T(8,128)S(1)}, u32[]{:S(2)}, u32[]{:S(2)}) collective-permute-start(f32[1,5,64,64]{3,2,1,0:T(8,128)S(1)} %collective-permute-done.9), channel_id=1, source_target_pairs={{0,15},{1,0},{2,1},{3,2},{4,3},{5,4},{6,5},{7,6},{8,7},{9,8},{10,9... | collective-permute-start | bytes 245768 | tf_op jit(solution)/shard_map/ppermute | solution.py:25
  263.4 3.0 collective-permute-done.10
  266.4 4.4 %collective-permute-start.13 = (f32[1,5,64,64]{3,2,1,0:T(8,128)S(1)}, f32[1,5,64,64]{3,2,1,0:T(8,128)S(1)}, u32[]{:S(2)}, u32[]{:S(2)}) collective-permute-start(f32[1,5,64,64]{3,2,1,0:T(8,128)S(1)} %collective-permute-done.11), channel_id=1, source_target_pairs={{0,15},{1,0},{2,1},{3,2},{4,3},{5,4},{6,5},{7,6},{8,7},{9,8},{10,9... | collective-permute-start | bytes 245768 | tf_op jit(solution)/shard_map/ppermute | solution.py:25
  270.9 3.1 collective-permute-done.12
  273.9 4.4 %collective-permute-start.15 = (f32[1,5,64,64]{3,2,1,0:T(8,128)S(1)}, f32[1,5,64,64]{3,2,1,0:T(8,128)S(1)}, u32[]{:S(2)}, u32[]{:S(2)}) collective-permute-start(f32[1,5,64,64]{3,2,1,0:T(8,128)S(1)} %collective-permute-done.13), channel_id=1, source_target_pairs={{0,15},{1,0},{2,1},{3,2},{4,3},{5,4},{6,5},{7,6},{8,7},{9,8},{10,9... | collective-permute-start | bytes 245768 | tf_op jit(solution)/shard_map/ppermute | solution.py:25
  278.4 3.1 collective-permute-done.14
  281.5 4.4 %collective-permute-start.17 = (f32[1,5,64,64]{3,2,1,0:T(8,128)S(1)}, f32[1,5,64,64]{3,2,1,0:T(8,128)S(1)}, u32[]{:S(2)}, u32[]{:S(2)}) collective-permute-start(f32[1,5,64,64]{3,2,1,0:T(8,128)S(1)} %collective-permute-done.15), channel_id=1, source_target_pairs={{0,15},{1,0},{2,1},{3,2},{4,3},{5,4},{6,5},{7,6},{8,7},{9,8},{10,9... | collective-permute-start | bytes 245768 | tf_op jit(solution)/shard_map/ppermute | solution.py:25
  285.9 2.9 collective-permute-done.16
  289.2 7.4 %collective-permute-done.18 = f32[1,5,64,64]{3,2,1,0:T(8,128)S(1)} collective-permute-done((f32[1,5,64,64]{3,2,1,0:T(8,128)S(1)}, f32[1,5,64,64]{3,2,1,0:T(8,128)S(1)}, u32[]{:S(2)}, u32[]{:S(2)}) %collective-permute-start.18) | collective-permute-done | bytes 81952 | tf_op jit(solution)/shard_map/ppermute | solution.py:22
  301.4 3.0 fusion.61
  311.6 4.4 %fusion.65 = bf16[4,128,512]{2,1,0:T(8,128)(2,1)} fusion(f32[4,128,258]{1,2,0:T(8,128)} %convolution_bitcast_fusion.2, f32[4,128,512]{2,1,0:T(8,128)} %slice.198, f32[128,512]{1,0:T(8,128)S(1)} %max.70, s32[258]{0:T(512)S(1)} %iota_multiply_fusion), kind=kOutput, calls=%fused_computation.101 | convolution fusion | flops 814365696 | bytes 2364424 | tf_op jit(solution)/shard_map/ciw,jw->cij/dot_general | solution.py:74
  (147 shorter events, 58.7 us)
Async XLA Ops:
  6.8 21.2 %all-to-all-start = ((bf16[16,2,5]{2,1,0:T(2,128)(2,1)}), bf16[16,2,5]{2,1,0:T(2,128)(2,1)S(1)}, u32[]{:S(2)}, u32[]{:S(2)}) async-start(bf16[16,2,5]{2,1,0:T(2,128)(2,1)} %broadcast_select_fusion.1), calls=%async_computation | async-start | bytes 16384 | tf_op jit(solution)/shard_map/all_to_all | solution.py:141
  28.0 84.2 %all-to-all-start.1 = ((bf16[32,4,16384]{2,1,0:T(4,128)(2,1)}), bf16[32,4,16384]{2,1,0:T(4,128)(2,1)}, u32[]{:S(2)}, u32[]{:S(2)}) async-start(bf16[32,4,16384]{2,1,0:T(4,128)(2,1)} %broadcast_select_fusion), calls=%async_computation.1 | async-start | bytes 8388608 | tf_op jit(solution)/shard_map/all_to_all | solution.py:140
  121.2 10.9 %copy-start.12 = (f32[16,1,128,128]{3,0,2,1:T(8,128)S(1)}, f32[16,1,128,128]{3,0,2,1:T(8,128)}, u32[]{:S(2)}) copy-start(f32[16,1,128,128]{3,0,2,1:T(8,128)} %fusion.58) | copy-start | bytes 3145732
  137.6 1.7 copy-start
  137.6 1.7 copy-start.2
  142.9 14.5 %collective-permute-start = (f32[5,512,22]{1,2,0:T(8,128)}, f32[5,512,22]{1,2,0:T(8,128)}, u32[]{:S(2)}, u32[]{:S(2)}) collective-permute-start(f32[5,512,22]{1,2,0:T(8,128)} %copy.124), channel_id=1, source_target_pairs={{0,2},{2,4},{4,6},{6,8},{8,10},{10,12},{12,14},{1,3},{3,5},{5,7},{... | collective-permute-start | bytes 675848 | tf_op jit(solution)/shard_map/ppermute | solution.py:37
  154.1 17.3 %collective-permute-start.1 = (f32[5,512,22]{1,2,0:T(8,128)}, f32[5,512,22]{1,2,0:T(8,128)}, u32[]{:S(2)}, u32[]{:S(2)}) collective-permute-start(f32[5,512,22]{1,2,0:T(8,128)} %copy.125), channel_id=1, source_target_pairs={{2,0},{4,2},{6,4},{8,6},{10,8},{12,10},{14,12},{3,1},{5,3},{7,5},{... | collective-permute-start | bytes 675848 | tf_op jit(solution)/shard_map/ppermute | solution.py:40
  173.8 15.4 %copy-start.1 = (f32[1,5,128,128]{3,0,2,1:T(1,128)S(1)}, f32[1,5,128,128]{3,0,2,1:T(1,128)}, u32[]{:S(2)}) copy-start(f32[1,5,128,128]{3,0,2,1:T(1,128)} %copy-done) | copy-start | bytes 983044
  173.8 15.4 %copy-start.3 = (f32[1,5,128,128]{3,0,2,1:T(1,128)S(1)}, f32[1,5,128,128]{3,0,2,1:T(1,128)}, u32[]{:S(2)}) copy-start(f32[1,5,128,128]{3,0,2,1:T(1,128)} %copy-done.2) | copy-start | bytes 983044
  173.8 15.4 %copy-start.5 = (f32[1,5,128,128]{3,0,2,1:T(1,128)S(1)}, f32[1,5,128,128]{3,0,2,1:T(1,128)}, u32[]{:S(2)}) copy-start(f32[1,5,128,128]{3,0,2,1:T(1,128)} %copy-done.4) | copy-start | bytes 983044
  173.8 15.4 %copy-start.7 = (f32[1,5,128,128]{3,0,2,1:T(1,128)S(1)}, f32[1,5,128,128]{3,0,2,1:T(1,128)}, u32[]{:S(2)}) copy-start(f32[1,5,128,128]{3,0,2,1:T(1,128)} %copy-done.6) | copy-start | bytes 983044
  173.8 15.4 %copy-start.9 = (f32[1,5,128,128]{3,0,2,1:T(1,128)S(1)}, f32[1,5,128,128]{3,0,2,1:T(1,128)}, u32[]{:S(2)}) copy-start(f32[1,5,128,128]{3,0,2,1:T(1,128)} %copy-done.8) | copy-start | bytes 983044
  173.8 15.4 %copy-start.11 = (f32[1,5,128,128]{3,0,2,1:T(1,128)S(1)}, f32[1,5,128,128]{3,0,2,1:T(1,128)}, u32[]{:S(2)}) copy-start(f32[1,5,128,128]{3,0,2,1:T(1,128)} %copy-done.10) | copy-start | bytes 983044
  186.6 3.5 %collective-permute-start.2 = (f32[5,22,556]{2,1,0:T(8,128)S(1)}, f32[5,22,556]{2,1,0:T(8,128)S(1)}, u32[]{:S(2)}, u32[]{:S(2)}) collective-permute-start(f32[5,22,556]{2,1,0:T(8,128)S(1)} %get-tuple-element.11), channel_id=1, source_target_pairs={{0,1},{2,3},{4,5},{6,7},{8,9},{10,11},{12,13},{14,15},{16,17},{18,... | collective-permute-start | bytes 733928 | tf_op jit(solution)/shard_map/ppermute | solution.py:37
  187.9 3.5 %collective-permute-start.3 = (f32[5,22,556]{2,1,0:T(8,128)S(1)}, f32[5,22,556]{2,1,0:T(8,128)S(1)}, u32[]{:S(2)}, u32[]{:S(2)}) collective-permute-start(f32[5,22,556]{2,1,0:T(8,128)S(1)} %get-tuple-element.12), channel_id=1, source_target_pairs={{1,0},{3,2},{5,4},{7,6},{9,8},{11,10},{13,12},{15,14},{17,16},{19,... | collective-permute-start | bytes 733928 | tf_op jit(solution)/shard_map/ppermute | solution.py:40
  190.0 13.9 %copy-start.16 = (f32[276,276]{1,0:T(8,128)S(1)}, f32[276,276]{1,0:T(8,128)}, u32[]{:S(2)}) copy-start(f32[276,276]{1,0:T(8,128)} %and_convert_fusion) | copy-start | bytes 914116
  218.5 25.2 %collective-permute-start.4 = (f32[1,5,64,64]{3,2,1,0:T(8,128)S(1)}, f32[1,5,64,64]{3,2,1,0:T(8,128)S(1)}, u32[]{:S(2)}, u32[]{:S(2)}) collective-permute-start(f32[1,5,64,64]{3,2,1,0:T(8,128)S(1)} %slice_bitcast_fusion), channel_id=1, source_target_pairs={{0,1},{1,2},{2,3},{3,4},{4,5},{5,6},{6,7},{7,8},{8,9},{9,10},{10,1... | collective-permute-start | bytes 245768 | tf_op jit(solution)/shard_map/ppermute | solution.py:22
  219.7 24.1 %collective-permute-start.5 = (f32[1,5,64,64]{3,2,1,0:T(8,128)S(1)}, f32[1,5,64,64]{3,2,1,0:T(8,128)S(1)}, u32[]{:S(2)}, u32[]{:S(2)}) collective-permute-start(f32[1,5,64,64]{3,2,1,0:T(8,128)S(1)} %slice_bitcast_fusion), channel_id=1, source_target_pairs={{0,15},{1,0},{2,1},{3,2},{4,3},{5,4},{6,5},{7,6},{8,7},{9,8},{10,9... | collective-permute-start | bytes 245768 | tf_op jit(solution)/shard_map/ppermute | solution.py:25
  243.8 7.6 %collective-permute-start.6 = (f32[1,5,64,64]{3,2,1,0:T(8,128)S(1)}, f32[1,5,64,64]{3,2,1,0:T(8,128)S(1)}, u32[]{:S(2)}, u32[]{:S(2)}) collective-permute-start(f32[1,5,64,64]{3,2,1,0:T(8,128)S(1)} %collective-permute-done.4), channel_id=1, source_target_pairs={{0,1},{1,2},{2,3},{3,4},{4,5},{5,6},{6,7},{7,8},{8,9},{9,10},{10,1... | collective-permute-start | bytes 245768 | tf_op jit(solution)/shard_map/ppermute | solution.py:22
  243.8 7.5 %collective-permute-start.7 = (f32[1,5,64,64]{3,2,1,0:T(8,128)S(1)}, f32[1,5,64,64]{3,2,1,0:T(8,128)S(1)}, u32[]{:S(2)}, u32[]{:S(2)}) collective-permute-start(f32[1,5,64,64]{3,2,1,0:T(8,128)S(1)} %collective-permute-done.5), channel_id=1, source_target_pairs={{0,15},{1,0},{2,1},{3,2},{4,3},{5,4},{6,5},{7,6},{8,7},{9,8},{10,9... | collective-permute-start | bytes 245768 | tf_op jit(solution)/shard_map/ppermute | solution.py:25
  251.4 7.4 %collective-permute-start.8 = (f32[1,5,64,64]{3,2,1,0:T(8,128)S(1)}, f32[1,5,64,64]{3,2,1,0:T(8,128)S(1)}, u32[]{:S(2)}, u32[]{:S(2)}) collective-permute-start(f32[1,5,64,64]{3,2,1,0:T(8,128)S(1)} %collective-permute-done.6), channel_id=1, source_target_pairs={{0,1},{1,2},{2,3},{3,4},{4,5},{5,6},{6,7},{7,8},{8,9},{9,10},{10,1... | collective-permute-start | bytes 245768 | tf_op jit(solution)/shard_map/ppermute | solution.py:22
  251.4 7.4 %collective-permute-start.9 = (f32[1,5,64,64]{3,2,1,0:T(8,128)S(1)}, f32[1,5,64,64]{3,2,1,0:T(8,128)S(1)}, u32[]{:S(2)}, u32[]{:S(2)}) collective-permute-start(f32[1,5,64,64]{3,2,1,0:T(8,128)S(1)} %collective-permute-done.7), channel_id=1, source_target_pairs={{0,15},{1,0},{2,1},{3,2},{4,3},{5,4},{6,5},{7,6},{8,7},{9,8},{10,9... | collective-permute-start | bytes 245768 | tf_op jit(solution)/shard_map/ppermute | solution.py:25
  258.8 7.5 %collective-permute-start.10 = (f32[1,5,64,64]{3,2,1,0:T(8,128)S(1)}, f32[1,5,64,64]{3,2,1,0:T(8,128)S(1)}, u32[]{:S(2)}, u32[]{:S(2)}) collective-permute-start(f32[1,5,64,64]{3,2,1,0:T(8,128)S(1)} %collective-permute-done.8), channel_id=1, source_target_pairs={{0,1},{1,2},{2,3},{3,4},{4,5},{5,6},{6,7},{7,8},{8,9},{9,10},{10,1... | collective-permute-start | bytes 245768 | tf_op jit(solution)/shard_map/ppermute | solution.py:22
  258.8 7.5 %collective-permute-start.11 = (f32[1,5,64,64]{3,2,1,0:T(8,128)S(1)}, f32[1,5,64,64]{3,2,1,0:T(8,128)S(1)}, u32[]{:S(2)}, u32[]{:S(2)}) collective-permute-start(f32[1,5,64,64]{3,2,1,0:T(8,128)S(1)} %collective-permute-done.9), channel_id=1, source_target_pairs={{0,15},{1,0},{2,1},{3,2},{4,3},{5,4},{6,5},{7,6},{8,7},{9,8},{10,9... | collective-permute-start | bytes 245768 | tf_op jit(solution)/shard_map/ppermute | solution.py:25
  266.4 7.5 %collective-permute-start.12 = (f32[1,5,64,64]{3,2,1,0:T(8,128)S(1)}, f32[1,5,64,64]{3,2,1,0:T(8,128)S(1)}, u32[]{:S(2)}, u32[]{:S(2)}) collective-permute-start(f32[1,5,64,64]{3,2,1,0:T(8,128)S(1)} %collective-permute-done.10), channel_id=1, source_target_pairs={{0,1},{1,2},{2,3},{3,4},{4,5},{5,6},{6,7},{7,8},{8,9},{9,10},{10,1... | collective-permute-start | bytes 245768 | tf_op jit(solution)/shard_map/ppermute | solution.py:22
  266.4 7.5 %collective-permute-start.13 = (f32[1,5,64,64]{3,2,1,0:T(8,128)S(1)}, f32[1,5,64,64]{3,2,1,0:T(8,128)S(1)}, u32[]{:S(2)}, u32[]{:S(2)}) collective-permute-start(f32[1,5,64,64]{3,2,1,0:T(8,128)S(1)} %collective-permute-done.11), channel_id=1, source_target_pairs={{0,15},{1,0},{2,1},{3,2},{4,3},{5,4},{6,5},{7,6},{8,7},{9,8},{10,9... | collective-permute-start | bytes 245768 | tf_op jit(solution)/shard_map/ppermute | solution.py:25
  273.9 7.5 %collective-permute-start.14 = (f32[1,5,64,64]{3,2,1,0:T(8,128)S(1)}, f32[1,5,64,64]{3,2,1,0:T(8,128)S(1)}, u32[]{:S(2)}, u32[]{:S(2)}) collective-permute-start(f32[1,5,64,64]{3,2,1,0:T(8,128)S(1)} %collective-permute-done.12), channel_id=1, source_target_pairs={{0,1},{1,2},{2,3},{3,4},{4,5},{5,6},{6,7},{7,8},{8,9},{9,10},{10,1... | collective-permute-start | bytes 245768 | tf_op jit(solution)/shard_map/ppermute | solution.py:22
  273.9 7.5 %collective-permute-start.15 = (f32[1,5,64,64]{3,2,1,0:T(8,128)S(1)}, f32[1,5,64,64]{3,2,1,0:T(8,128)S(1)}, u32[]{:S(2)}, u32[]{:S(2)}) collective-permute-start(f32[1,5,64,64]{3,2,1,0:T(8,128)S(1)} %collective-permute-done.13), channel_id=1, source_target_pairs={{0,15},{1,0},{2,1},{3,2},{4,3},{5,4},{6,5},{7,6},{8,7},{9,8},{10,9... | collective-permute-start | bytes 245768 | tf_op jit(solution)/shard_map/ppermute | solution.py:25
  281.5 7.4 %collective-permute-start.16 = (f32[1,5,64,64]{3,2,1,0:T(8,128)S(1)}, f32[1,5,64,64]{3,2,1,0:T(8,128)S(1)}, u32[]{:S(2)}, u32[]{:S(2)}) collective-permute-start(f32[1,5,64,64]{3,2,1,0:T(8,128)S(1)} %collective-permute-done.14), channel_id=1, source_target_pairs={{0,1},{1,2},{2,3},{3,4},{4,5},{5,6},{6,7},{7,8},{8,9},{9,10},{10,1... | collective-permute-start | bytes 245768 | tf_op jit(solution)/shard_map/ppermute | solution.py:22
  281.5 7.7 %collective-permute-start.17 = (f32[1,5,64,64]{3,2,1,0:T(8,128)S(1)}, f32[1,5,64,64]{3,2,1,0:T(8,128)S(1)}, u32[]{:S(2)}, u32[]{:S(2)}) collective-permute-start(f32[1,5,64,64]{3,2,1,0:T(8,128)S(1)} %collective-permute-done.15), channel_id=1, source_target_pairs={{0,15},{1,0},{2,1},{3,2},{4,3},{5,4},{6,5},{7,6},{8,7},{9,8},{10,9... | collective-permute-start | bytes 245768 | tf_op jit(solution)/shard_map/ppermute | solution.py:25
  288.9 7.6 %collective-permute-start.18 = (f32[1,5,64,64]{3,2,1,0:T(8,128)S(1)}, f32[1,5,64,64]{3,2,1,0:T(8,128)S(1)}, u32[]{:S(2)}, u32[]{:S(2)}) collective-permute-start(f32[1,5,64,64]{3,2,1,0:T(8,128)S(1)} %collective-permute-done.16), channel_id=1, source_target_pairs={{0,1},{1,2},{2,3},{3,4},{4,5},{5,6},{6,7},{7,8},{8,9},{9,10},{10,1... | collective-permute-start | bytes 245768 | tf_op jit(solution)/shard_map/ppermute | solution.py:22
  301.4 7.1 %copy-start.13 = (f32[4,2,64,8,64]{4,2,0,1,3:T(8,128)S(1)}, f32[4,2,64,8,64]{4,2,0,1,3:T(8,128)}, u32[]{:S(2)}) copy-start(f32[4,2,64,8,64]{4,2,0,1,3:T(8,128)} %slice.255) | copy-start | bytes 3145732
  (6 other events, 10.0 us)
